TPU v7x, 32 devices: a whole 2x2x4 slice. The times are simulated.
32 devices in a mesh: space: 4 (over y, x), chan: 8 (over z, core).
Axes of the slice: x: 2, y: 2, z: 4, core: 2. Of those that a mesh axis runs over, the one named last changes fastest.
Arguments:
- inputs: bfloat16 [256, 16, 1024], P('chan', 'space'), may hold values from -6 to 6
- weight: bfloat16 [27, 256, 256], P(None, None, 'chan'), may hold values from -0.078125 to 0.078125
- bias_term: float32 [256], P('chan'), may hold values from -1 to 1
- output_grad: bfloat16 [256, 16, 1024], P('chan', 'space'), may hold values from -6 to 6
Outputs:
- outputs: bfloat16 [256, 16, 1024], P('chan', 'space')
- input_grad: bfloat16 [256, 16, 1024], P('chan', 'space')
- weight_grad: float32 [27, 256, 256], P(None, None, 'chan')
- bias_grad: float32 [256], P('chan')
All inputs are finite; a program needn't handle non-finite values.
Results may differ from a plain program's by a relative error of at most 0.001.
Values may be sent and summed in bfloat16 or wider, within the bound.
No kernel may reach another device: no remote copies, remote signals or barrier semaphores. Data moves between devices by JAX's collectives and lax.ppermute only.
A program may use at most 128 MiB of HBM per device.

v0:
```python
import math

import jax
import jax.numpy as jnp
from jax import lax
from jax.sharding import PartitionSpec as P

W = 64


tap_offsets = tuple(
    (
        (depth_step, row_step, column_step)
        for depth_step in (-1, 0, 1)
        for row_step in (-1, 0, 1)
        for column_step in (-1, 0, 1)
    )
)


def padded_2(array, sides, width):
    for axis, dim in sides:
        devices, length = (lax.axis_size(axis), array.shape[dim])
        up = [(i, (i + 1) % devices) for i in range(devices - 1)]
        down = [(j, i) for i, j in up]
        last = lax.slice_in_dim(array, length - width, length, axis=dim)
        first = lax.slice_in_dim(array, 0, width, axis=dim)
        before = lax.ppermute(last, axis, up)
        after = lax.ppermute(first, axis, down)
        array = jnp.concatenate([before, array, after], axis=dim)
    return array


def shift_cells(field, row_step, column_step):
    length_flat = field.shape[-1]
    pad_width = W + 1
    widths = [(0, 0)] * (field.ndim - 1) + [(pad_width, pad_width)]
    padded = jnp.pad(field, widths)
    first_index = pad_width + row_step * W + column_step
    shifted = lax.slice_in_dim(padded, first_index, first_index + length_flat, axis=field.ndim - 1)
    column = jnp.arange(length_flat, dtype=jnp.int32) % W
    inside = (column + column_step >= 0) & (column + column_step < W)
    return jnp.where(inside, shifted, jnp.zeros_like(shifted))


def outer_planes(field):
    return jnp.concatenate([field[:, :1], field[:, -1:]], axis=1)


def attach_rims(field, rims):
    return jnp.concatenate([rims[:, :1], field, rims[:, 3:]], axis=1)


def body(inputs, weight, bias_term, output_grad):
    taps_total = weight.shape[0]
    channels_in = weight.shape[1]
    block_out = weight.shape[2]
    block_in = inputs.shape[0]
    depth_cells = inputs.shape[1]
    plane_cells = inputs.shape[2]
    grad_scale = 1.0 / math.sqrt(lax.axis_size("space") * depth_cells * plane_cells)
    own_rims = padded_2(outer_planes(inputs), (("space", 1),), 1)
    rimmed = attach_rims(inputs, own_rims)
    gathered = lax.all_gather(rimmed, "chan", axis=0, tiled=True)
    gathered_flat = gathered.reshape(channels_in, (depth_cells + 2) * plane_cells)
    forward_weight = jnp.transpose(weight, (0, 2, 1)).reshape(taps_total * block_out, channels_in)
    stacked = jnp.dot(forward_weight, gathered_flat, preferred_element_type=jnp.float32)
    stacked = stacked.reshape(taps_total, block_out, depth_cells + 2, plane_cells)
    forward = jnp.zeros((block_out, depth_cells, plane_cells), jnp.float32)
    for tap_index, (depth_step, row_step, column_step) in enumerate(tap_offsets):
        forward = forward + shift_cells(
            stacked[tap_index, :, 1 + depth_step : 1 + depth_step + depth_cells],
            row_step,
            column_step,
        )
    outputs = (forward + bias_term[:, None, None]).astype(jnp.bfloat16)
    grad_rimmed = padded_2(output_grad, (("space", 1),), 1)
    grad_wide = jnp.pad(output_grad, ((0, 0), (2, 2), (0, 0)))
    placed = jnp.stack(
        [
            shift_cells(
                grad_wide[:, 1 - depth_step : 1 - depth_step + depth_cells + 2],
                -row_step,
                -column_step,
            )
            for depth_step, row_step, column_step in tap_offsets
        ]
    )
    placed = placed.reshape(taps_total * block_out, (depth_cells + 2) * plane_cells)
    weight_part = lax.dot_general(
        gathered_flat, placed, (((1,), (1,)), ((), ())), preferred_element_type=jnp.float32
    )
    weight_part = (
        jnp.transpose(weight_part.reshape(channels_in, taps_total, block_out), (1, 0, 2))
        * grad_scale
    )
    bias_part = jnp.sum(output_grad.astype(jnp.float32), axis=(1, 2)) * grad_scale
    weight_grad, bias_grad = lax.psum((weight_part, bias_part), "space")
    spread = jnp.stack(
        [
            shift_cells(
                grad_rimmed[:, 1 - depth_step : 1 - depth_step + depth_cells],
                -row_step,
                -column_step,
            )
            for depth_step, row_step, column_step in tap_offsets
        ]
    )
    spread = spread.reshape(taps_total * block_out, depth_cells * plane_cells)
    backward_weight = jnp.transpose(weight, (1, 0, 2)).reshape(channels_in, taps_total * block_out)
    summed = lax.psum_scatter(
        jnp.dot(backward_weight, spread, preferred_element_type=jnp.float32),
        "chan",
        scatter_dimension=0,
        tiled=True,
    )
    input_grad = summed.astype(jnp.bfloat16).reshape(block_in, depth_cells, plane_cells)
    return (outputs, input_grad, weight_grad, bias_grad)


def solution(mesh):
    placed = (P("chan", "space", None), P(None, None, "chan"), P("chan"), P("chan", "space", None))
    return jax.shard_map(
        body,
        mesh=mesh,
        in_specs=placed,
        out_specs=(
            P("chan", "space", None),
            P("chan", "space", None),
            P(None, None, "chan"),
            P("chan"),
        ),
        check_vma=False,
    )
```

profile of v0, /device:TPU:0, one launch (start us, length us, event | category | flops | bytes accessed | tf_op | source)
XLA Modules:
  0.0 213.4 jit_solution(16528405586227326812)
XLA Ops:
  7.2 1.1 copy.19
  8.4 4.8 %collective-permute-start = (bf16[32,1,1024]{2,0,1:T(8,128)(2,1)S(1)}, bf16[32,1,1024]{2,0,1:T(8,128)(2,1)S(1)}, u32[]{:S(2)}, u32[]{:S(2)}) collective-permute-start(bf16[32,1,1024]{2,0,1:T(8,128)(2,1)S(1)} %get-tuple-element.47), channel_id=1, source_target_pairs={{0,8},{8,16},{16,24},{1,9},{9,17},{17,25},{2,10},{10,18},{18,26},{... | collective-permute-start | bytes 196616 | tf_op jit(solution)/shard_map/ppermute | solution.py:28
  13.2 1.3 collective-permute-start.1
  14.5 1.3 fusion.150
  15.8 1.3 collective-permute-start.2
  17.1 5.2 %collective-permute-start.3 = (bf16[32,1,1024]{2,1,0:T(2,128)(2,1)S(1)}, bf16[32,1,1024]{2,1,0:T(2,128)(2,1)S(1)}, u32[]{:S(2)}, u32[]{:S(2)}) collective-permute-start(bf16[32,1,1024]{2,1,0:T(2,128)(2,1)S(1)} %get-tuple-element.45), channel_id=1, source_target_pairs={{0,8},{8,16},{16,24},{1,9},{9,17},{17,25},{2,10},{10,18},{18,26},{... | collective-permute-start | bytes 196616 | tf_op jit(solution)/shard_map/ppermute | solution.py:28
  22.3 1.0 copy.23
  23.3 1.3 convert_reduce_fusion
  24.8 0.9 fusion.66
  25.7 0.9 fusion.69
  26.6 0.9 fusion.72
  27.6 0.9 fusion.75
  29.3 0.9 fusion.78
  30.2 0.9 fusion.81
  31.1 1.0 fusion.84
  32.1 0.9 fusion.87
  33.0 10.9 %psum.15 = f32[32]{0:T(128)} all-reduce(f32[32]{0:T(128)S(1)} %broadcast_multiply_fusion), channel_id=1, replica_groups=mesh['space'=4,'chan'=8] {'space'}, use_global_device_ids=true, to_apply=%region_3.4 | all-reduce | flops 32 | bytes 256 | tf_op jit(solution)/shard_map/psum | solution.py:98
  52.5 7.7 %copy.28 = bf16[108,8,4,1024]{3,1,2,0:T(8,128)(2,1)} copy(bf16[108,8,4,1024]{3,2,1,0:T(4,128)(2,1)S(1)} %bitcast.273) | data formatting | bytes 14155776
  60.2 7.6 %convolution_bitcast_fusion.1 = f32[256,4096]{0,1:T(8,128)} fusion(bf16[864,4096]{1,0:T(8,128)(2,1)} %bitcast.274, bf16[256,864]{0,1:T(8,128)(2,1)S(1)} %bitcast.271), kind=kOutput, calls=%fused_computation.1 | convolution fusion | flops 1811939328 | bytes 11714560 | tf_op jit(solution)/shard_map/dot_general | solution.py:112
  67.8 5.7 %copy.26 = f32[256,4096]{1,0:T(8,128)} copy(f32[256,4096]{0,1:T(8,128)} %convolution_bitcast_fusion.1) | data formatting | bytes 8388608
  73.6 0.9 fusion.90
  74.5 1.0 fusion.93
  75.5 0.9 fusion.96
  76.4 0.9 fusion.99
  78.2 1.0 fusion.102
  79.1 0.9 fusion.105
  80.0 0.9 fusion.108
  81.0 0.9 fusion.111
  81.9 0.9 fusion.114
  82.8 0.9 fusion.117
  83.8 0.9 fusion.120
  84.7 0.9 fusion.123
  85.6 0.8 bitcast_dynamic-update-slice_fusion
  86.5 0.9 fusion.126
  87.4 0.9 fusion.129
  88.3 0.9 fusion.132
  89.3 1.0 fusion.135
  90.2 4.7 %copy.22 = bf16[256,6,1024]{0,2,1:T(8,128)(2,1)} copy(bf16[256,6,1024]{2,0,1:T(8,128)(2,1)} %all-gather.2.cloned.1.call-done) | data formatting | bytes 6291456 | tf_op jit(solution)/shard_map/all_gather | solution.py:64
  95.0 10.8 %convolution_bitcast_fusion = f32[864,6144]{1,0:T(8,128)} fusion(bf16[256,6144]{0,1:T(8,128)(2,1)} %bitcast.272, bf16[864,256]{1,0:T(8,128)(2,1)S(1)} %bitcast.270), kind=kOutput, calls=%fused_computation | convolution fusion | flops 2717908992 | bytes 24821760 | tf_op jit(solution)/shard_map/dot_general | solution.py:67
  105.7 27.9 %reshape.33 = f32[27,32,6,1024]{3,2,1,0:T(8,128)} reshape(f32[864,6144]{1,0:T(8,128)} %convolution_bitcast_fusion) | data formatting | bytes 42467328 | tf_op jit(solution)/shard_map/reshape | solution.py:68
  133.6 3.5 %slice_bitcast_fusion.25 = (f32[32,4,1024]{2,1,0:T(4,128)S(1)}, f32[32,4,1024]{2,1,0:T(4,128)S(1)}, f32[32,4,1024]{2,1,0:T(4,128)S(1)}, f32[32,4,1024]{2,1,0:T(4,128)S(1)}, f32[32,4,1024]{2,1,0:T(4,128)S(1)}) fusion(f32[27,32,6,1024]{3,2,1,0:T(8,128)} %reshape.33), kind=kLoop, calls=%fused_computation.112 | loop fusion | bytes 5242880 | tf_op jit(solution)/shard_map/squeeze | solution.py:72
  137.1 11.6 %slice_bitcast_fusion.26 = (f32[32,4,1024]{2,1,0:T(4,128)}, f32[32,4,1024]{2,1,0:T(4,128)}, f32[32,4,1024]{2,1,0:T(4,128)}, f32[32,4,1024]{2,1,0:T(4,128)}, f32[...) fusion(f32[27,32,6,1024]{3,2,1,0:T(8,128)} %reshape.33), kind=kLoop, calls=%fused_computation.113 | loop fusion | bytes 19922944 | tf_op jit(solution)/shard_map/squeeze | solution.py:72
  150.2 3.9 %fusion.8 = f32[27,256,32]{1,2,0:T(8,128)} fusion(bf16[27,32,6,1024]{3,1,2,0:T(8,128)(2,1)S(1)} %bitcast.277, bf16[256,6,1024]{2,0,1:T(8,128)(2,1)S(1)} %copy-done.3), kind=kOutput, calls=%fused_computation.6 | convolution fusion | flops 2718130176 | bytes 14647296 | tf_op jit(solution)/shard_map/dot_general | solution.py:90
  154.1 10.4 %add_convert_fusion = bf16[32,4,1024]{2,1,0:T(4,128)(2,1)} fusion(f32[32,4,1024]{2,1,0:T(4,128)S(1)} %get-tuple-element.37, f32[32,4,1024]{2,1,0:T(4,128)} %get-tuple-element.27, f32[32,4,1024]{2,1,0:T(4,128)} %get-tuple-element.17, f32[32,4,1024]{2,1,0:T(4,128)} %get-tuple-element.18, f32[27,32,6,1024]{3,2,1,0:T(8,128)} %reshape.33, ...), kind=kLoop, calls=%fused_computation.115 | loop fusion | flops 7208960 | bytes 14421120 | tf_op jit(solution)/shard_map/convert_element_type | solution.py:76
  164.5 1.5 copy.27
  166.0 1.2 copy.24
  167.3 37.4 %all-reduce.33.cloned.1.call-done = f32[27,256,32]{1,2,0:T(8,128)} async-done(((f32[27,256,32]{1,2,0:T(8,128)}), f32[27,256,32]{1,2,0:T(8,128)}) %all-reduce.33.cloned.1.call-update) | async-done | bytes 884752 | tf_op jit(solution)/shard_map/psum | solution.py:98
  204.7 2.2 %copy.82 = f32[27,256,32]{1,2,0:T(8,128)} copy(f32[27,256,32]{1,2,0:T(8,128)} %all-reduce.33.cloned.1.call-done) | data formatting | bytes 1769472
  (65 shorter events, 11.9 us)
Async XLA Ops:
  7.2 53.1 %copy-start = (bf16[27,256,32]{1,2,0:T(8,128)(2,1)S(1)}, bf16[27,256,32]{1,2,0:T(8,128)(2,1)}, u32[]{:S(2)}) copy-start(bf16[27,256,32]{1,2,0:T(8,128)(2,1)} %param.5) | copy-start | bytes 1327108
  7.2 37.8 %copy-start.2 = (bf16[32,4,1024]{2,1,0:T(4,128)(2,1)S(1)}, bf16[32,4,1024]{2,1,0:T(4,128)(2,1)}, u32[]{:S(2)}) copy-start(bf16[32,4,1024]{2,1,0:T(4,128)(2,1)} %param.7) | copy-start | bytes 786436
  7.2 83.0 %all-gather.2.cloned.1.call-start = ((), (), s32[]{:S(2)}) async-start(), calls=%async_computation.1 | async-start | bytes 3538944 | tf_op jit(solution)/shard_map/all_gather | solution.py:64
  8.4 35.6 %collective-permute-start = (bf16[32,1,1024]{2,0,1:T(8,128)(2,1)S(1)}, bf16[32,1,1024]{2,0,1:T(8,128)(2,1)S(1)}, u32[]{:S(2)}, u32[]{:S(2)}) collective-permute-start(bf16[32,1,1024]{2,0,1:T(8,128)(2,1)S(1)} %get-tuple-element.47), channel_id=1, source_target_pairs={{0,8},{8,16},{16,24},{1,9},{9,17},{17,25},{2,10},{10,18},{18,26},{... | collective-permute-start | bytes 196616 | tf_op jit(solution)/shard_map/ppermute | solution.py:28
  13.2 30.7 %collective-permute-start.1 = (bf16[32,1,1024]{2,0,1:T(8,128)(2,1)S(1)}, bf16[32,1,1024]{2,0,1:T(8,128)(2,1)S(1)}, u32[]{:S(2)}, u32[]{:S(2)}) collective-permute-start(bf16[32,1,1024]{2,0,1:T(8,128)(2,1)S(1)} %get-tuple-element.48), channel_id=1, source_target_pairs={{8,0},{16,8},{24,16},{9,1},{17,9},{25,17},{10,2},{18,10},{26,18},{... | collective-permute-start | bytes 196616 | tf_op jit(solution)/shard_map/ppermute | solution.py:29
  15.8 29.2 %collective-permute-start.2 = (bf16[32,1,1024]{2,1,0:T(2,128)(2,1)S(1)}, bf16[32,1,1024]{2,1,0:T(2,128)(2,1)S(1)}, u32[]{:S(2)}, u32[]{:S(2)}) collective-permute-start(bf16[32,1,1024]{2,1,0:T(2,128)(2,1)S(1)} %get-tuple-element.46), channel_id=1, source_target_pairs={{8,0},{16,8},{24,16},{9,1},{17,9},{25,17},{10,2},{18,10},{26,18},{... | collective-permute-start | bytes 196616 | tf_op jit(solution)/shard_map/ppermute | solution.py:29
  17.1 27.9 %collective-permute-start.3 = (bf16[32,1,1024]{2,1,0:T(2,128)(2,1)S(1)}, bf16[32,1,1024]{2,1,0:T(2,128)(2,1)S(1)}, u32[]{:S(2)}, u32[]{:S(2)}) collective-permute-start(bf16[32,1,1024]{2,1,0:T(2,128)(2,1)S(1)} %get-tuple-element.45), channel_id=1, source_target_pairs={{0,8},{8,16},{16,24},{1,9},{9,17},{17,25},{2,10},{10,18},{18,26},{... | collective-permute-start | bytes 196616 | tf_op jit(solution)/shard_map/ppermute | solution.py:28
  44.8 119.8 %reduce-scatter.4.cloned.1.call-start = ((), (), s32[]{:S(2)}) async-start(), calls=%async_computation.3 | async-start | bytes 4718592
  73.5 131.1 %all-reduce.33.cloned.1.call-start = ((), (), s32[]{:S(2)}) async-start(), calls=%async_computation.2 | async-start | bytes 1769472 | tf_op jit(solution)/shard_map/psum | solution.py:98
  133.6 15.1 %slice-start = ((s8[10616832]{0:T(1024)(128)(4,1)}), s8[4194304]{0:T(1024)(128)(4,1)S(1)}, s32[]{:S(2)}) async-start(s8[10616832]{0:T(1024)(128)(4,1)} %bitcast.276), calls=%async_computation.4 | async-start | bytes 8388608
  137.1 11.6 %copy-start.3 = (bf16[256,6,1024]{2,0,1:T(8,128)(2,1)S(1)}, bf16[256,6,1024]{2,0,1:T(8,128)(2,1)}, u32[]{:S(2)}) copy-start(bf16[256,6,1024]{2,0,1:T(8,128)(2,1)} %all-gather.2.cloned.1.call-done) | copy-start | bytes 9437188
  137.1 12.4 %slice-start.1 = ((s8[10616832]{0:T(1024)(128)(4,1)}), s8[4194304]{0:T(1024)(128)(4,1)S(1)}, s32[]{:S(2)}) async-start(s8[10616832]{0:T(1024)(128)(4,1)} %bitcast.276), calls=%async_computation.5 | async-start | bytes 8388608
  137.1 13.1 %slice-start.2 = ((s8[10616832]{0:T(1024)(128)(4,1)}), s8[2228224]{0:T(1024)(128)(4,1)S(1)}, s32[]{:S(2)}) async-start(s8[10616832]{0:T(1024)(128)(4,1)} %bitcast.276), calls=%async_computation.6 | async-start | bytes 4456448
  150.2 3.9 %copy-start.4 = (f32[32]{0:T(128)S(1)}, f32[32]{0:T(128)}, u32[]{:S(2)}) copy-start(f32[32]{0:T(128)} %param.6) | copy-start | bytes 388
  154.1 52.8 %copy-start.1 = (bf16[27,256,32]{1,2,0:T(8,128)(2,1)S(1)}, bf16[27,256,32]{1,2,0:T(8,128)(2,1)}, u32[]{:S(2)}) copy-start(bf16[27,256,32]{1,2,0:T(8,128)(2,1)} %param.5) | copy-start | bytes 1327108
Sparse Core Ops, SparseCore 0:
  44.9 38.5 all-gather.1
  85.7 48.8 reduce-scatter.3
  154.2 50.4 all-reduce.32
where the time goes:
time: 215 us; the launch traced here: 213 us
  local copies, waits for them, and re-layouts  71.1 us (33%)
  other arithmetic  44.8 us (21%)
  waiting for transfers between devices  37.5 us (17%)
  matrix products  22.2 us (10%)
  between operations  14 us (7%)
  starting transfers between devices  12.9 us (6%)
  blocking collectives  10.9 us (5%)
    psum x1, waiting for transfers between devices, body(): weight_grad, bias_grad = lax.psum((weight_part, bias_part), 'space')  37.4 us
    unnamed x53, other arithmetic  30.5 us
    reshape x1, local copies, waits for them, and re-layouts, body(): stacked.reshape(taps_total, block_out, depth_cells + 2, plane_cells)  27.9 us
    unnamed x23, local copies, waits for them, and re-layouts  22 us
    squeeze x2, local copies, waits for them, and re-layouts, body(): stacked[tap_index, :, 1 + depth_step:1 + depth_step + depth_cells]  15.1 us
    psum x1, blocking collectives, body(): weight_grad, bias_grad = lax.psum((weight_part, bias_part), 'space')  10.9 us
    dot_general x1, matrix products, body(): jnp.dot(forward_weight, gathered_flat, preferred_element_type=jnp.float32)  10.8 us
    convert_element_type x1, other arithmetic, body(): outputs = (forward + bias_term[:, None, None]).astype(jnp.bfloat16)  10.4 us
  transfers between devices with their start and end apart: 7, of which 1 were waited for; matrix products, arithmetic and copies ran while one was open for 62% of the time, Pallas kernels for 0%

commit v1 on v0

v1 whole, which is shorter than its diff:
```python
import math

import jax
import jax.numpy as jnp
from jax import lax
from jax.sharding import PartitionSpec as P

W = 64


def padded_2(array, sides, width):
    for axis, dim in sides:
        devices, length = (lax.axis_size(axis), array.shape[dim])
        up = [(i, (i + 1) % devices) for i in range(devices - 1)]
        down = [(j, i) for i, j in up]
        last = lax.slice_in_dim(array, length - width, length, axis=dim)
        first = lax.slice_in_dim(array, 0, width, axis=dim)
        before = lax.ppermute(last, axis, up)
        after = lax.ppermute(first, axis, down)
        array = jnp.concatenate([before, array, after], axis=dim)
    return array


def outer_planes(field):
    return jnp.concatenate([field[:, :1], field[:, -1:]], axis=1)


def attach_rims(field, rims):
    return jnp.concatenate([rims[:, :1], field, rims[:, 3:]], axis=1)


def volume(field):
    return field.reshape(1, field.shape[0], field.shape[1], field.shape[2] // W, W)


def body(inputs, weight, bias_term, output_grad):
    taps_total = weight.shape[0]
    channels_in = weight.shape[1]
    block_out = weight.shape[2]
    block_in = inputs.shape[0]
    depth_cells = inputs.shape[1]
    plane_cells = inputs.shape[2]
    rows = plane_cells // W
    grad_scale = 1.0 / math.sqrt(lax.axis_size("space") * depth_cells * plane_cells)
    own_rims = padded_2(outer_planes(inputs), (("space", 1),), 1)
    rimmed = attach_rims(inputs, own_rims)
    gathered = lax.all_gather(rimmed, "chan", axis=0, tiled=True)
    kernel = weight.reshape(3, 3, 3, channels_in, block_out)
    in_vol = volume(gathered)
    forward = lax.conv_general_dilated(
        in_vol,
        kernel,
        window_strides=(1, 1, 1),
        padding=((0, 0), (1, 1), (1, 1)),
        dimension_numbers=("NCDHW", "DHWIO", "NCDHW"),
        preferred_element_type=jnp.float32,
    )
    forward = forward.reshape(block_out, depth_cells, plane_cells)
    outputs = (forward + bias_term[:, None, None]).astype(jnp.bfloat16)

    grad_vol = volume(output_grad)
    filter_grad = lax.conv_general_dilated(
        in_vol.reshape(channels_in, 1, depth_cells + 2, rows, W),
        grad_vol.reshape(1, block_out, depth_cells, rows, W),
        window_strides=(1, 1, 1),
        padding=((0, 0), (1, 1), (1, 1)),
        dimension_numbers=("NCDHW", "IODHW", "NCDHW"),
        preferred_element_type=jnp.float32,
    )
    weight_part = jnp.transpose(filter_grad, (2, 3, 4, 0, 1)).reshape(taps_total * channels_in * block_out)
    bias_part = jnp.sum(output_grad.astype(jnp.float32), axis=(1, 2))
    reduced = lax.psum(jnp.concatenate([weight_part, bias_part]) * grad_scale, "space")
    weight_grad = reduced[: taps_total * channels_in * block_out].reshape(taps_total, channels_in, block_out)
    bias_grad = reduced[taps_total * channels_in * block_out :]

    grad_rimmed = padded_2(output_grad, (("space", 1),), 1)
    flipped = kernel[::-1, ::-1, ::-1]
    spread = lax.conv_general_dilated(
        volume(grad_rimmed),
        flipped,
        window_strides=(1, 1, 1),
        padding=((0, 0), (1, 1), (1, 1)),
        dimension_numbers=("NCDHW", "DHWOI", "NCDHW"),
        preferred_element_type=jnp.float32,
    )
    summed = lax.psum_scatter(
        spread.reshape(channels_in, depth_cells * plane_cells),
        "chan",
        scatter_dimension=0,
        tiled=True,
    )
    input_grad = summed.astype(jnp.bfloat16).reshape(block_in, depth_cells, plane_cells)
    return (outputs, input_grad, weight_grad, bias_grad)


def solution(mesh):
    placed = (P("chan", "space", None), P(None, None, "chan"), P("chan"), P("chan", "space", None))
    return jax.shard_map(
        body,
        mesh=mesh,
        in_specs=placed,
        out_specs=(
            P("chan", "space", None),
            P("chan", "space", None),
            P(None, None, "chan"),
            P("chan"),
        ),
        check_vma=False,
    )
```

time: 215 us -> 263 us (1.22); the launches traced: 213 us -> 258 us
  matrix products: 22.2 us -> 99.6 us
  other arithmetic: 44.8 us -> 4.18 us
  waiting for transfers between devices: 37.5 us -> 74 us
  local copies, waits for them, and re-layouts: 71.1 us -> 54 us
  blocking collectives: 10.9 us -> 0 us
    transpose x0 -> x1, matrix products: none -> 78.2 us  [body(): jnp.transpose(filter_grad, (2, 3, 4, 0, 1))]
    unnamed x4, waiting for transfers between devices: 0.07 us -> 44.9 us
    psum x1, waiting for transfers between devices: 37.4 us -> 4.18 us  [body(): lax.psum(jnp.concatenate([weight_part, bias_part]) * grad_scale, 'space')]
    unnamed x53 -> x0, other arithmetic: 30.5 us -> none
    dot_general x3 -> x0, matrix products: 22.2 us -> none  [the longest x1 10.8 us: body(): jnp.dot(forward_weight, gathered_flat, preferred_element_type=jnp.float32)]
    conv_general_dilated x0 -> x2, matrix products: none -> 21.5 us  [the longest x1 17.4 us: body(): lax.conv_general_dilated(in_vol, kernel, window_strides=(1, 1, 1), paddin...]
    all_gather x1, waiting for transfers between devices: 0.01 us -> 20.1 us  [body(): gathered = lax.all_gather(rimmed, 'chan', axis=0, tiled=True)]
    squeeze x2 -> x0, local copies, waits for them, and re-layouts: 15.1 us -> none  [body(): stacked[tap_index, :, 1 + depth_step:1 + depth_step + depth_cells]]
  transfers between devices with their start and end apart: 7 -> 7, of which waited for: 1 -> 5; matrix products, arithmetic and copies ran while one was open for 62% -> 25% of each run, Pallas kernels for 0% -> 0%
where the time goes in v1:
time: 263 us; the launch traced here: 258 us
  matrix products  99.6 us (38%)
  waiting for transfers between devices  74 us (28%)
  local copies, waits for them, and re-layouts  54 us (21%)
  between operations  14.2 us (5%)
  starting transfers between devices  12.3 us (5%)
  other arithmetic  4.18 us (2%)
    transpose x1, matrix products, body(): jnp.transpose(filter_grad, (2, 3, 4, 0, 1))  78.2 us
    unnamed x4, waiting for transfers between devices  44.9 us
    unnamed x26, local copies, waits for them, and re-layouts  20.6 us
    all_gather x1, waiting for transfers between devices, body(): gathered = lax.all_gather(rimmed, 'chan', axis=0, tiled=True)  20.1 us
    conv_general_dilated x1, matrix products, body(): lax.conv_general_dilated(in_vol, kernel, window_strides=(1, 1, 1), paddin...  17.4 us
    ppermute x2, starting transfers between devices, padded_2(): before = lax.ppermute(last, axis, up)  9.15 us
    conv_general_dilated x5, local copies, waits for them, and re-layouts, body(): lax.conv_general_dilated(volume(grad_rimmed), flipped, window_strides=(1,...  7.59 us
    reshape x5, local copies, waits for them, and re-layouts, volume(): field.reshape(1, field.shape[0], field.shape[1], field.shape[2] // W, W)  6.43 us
  transfers between devices with their start and end apart: 7, of which 5 were waited for; matrix products, arithmetic and copies ran while one was open for 25% of the time, Pallas kernels for 0%

profile of v1, /device:TPU:0, one launch (start us, length us, event | category | flops | bytes accessed | tf_op | source)
XLA Modules:
  0.0 258.3 jit_solution(15466908486924763451)
XLA Ops:
  7.2 1.1 copy.48
  8.4 4.8 %collective-permute-start = (bf16[32,1,1024]{2,0,1:T(8,128)(2,1)S(1)}, bf16[32,1,1024]{2,0,1:T(8,128)(2,1)S(1)}, u32[]{:S(2)}, u32[]{:S(2)}) collective-permute-start(bf16[32,1,1024]{2,0,1:T(8,128)(2,1)S(1)} %get-tuple-element.18), channel_id=1, source_target_pairs={{0,8},{8,16},{16,24},{1,9},{9,17},{17,25},{2,10},{10,18},{18,26},{... | collective-permute-start | bytes 196616 | tf_op jit(solution)/shard_map/ppermute | solution.py:18
  13.2 1.3 collective-permute-start.1
  14.5 0.6 collective-permute-done
  15.1 4.3 %collective-permute-done.1 = bf16[32,1,1024]{2,0,1:T(8,128)(2,1)S(1)} collective-permute-done((bf16[32,1,1024]{2,0,1:T(8,128)(2,1)S(1)}, bf16[32,1,1024]{2,0,1:T(8,128)(2,1)S(1)}, u32[]{:S(2)}, u32[]{:S(2)}) %collective-permute-start.1) | collective-permute-done | bytes 65568 | tf_op jit(solution)/shard_map/ppermute | solution.py:19
  19.4 0.8 pad_maximum_fusion.1
  20.2 1.3 fusion.31
  21.5 4.3 %collective-permute-start.2 = (bf16[32,1,1024]{2,1,0:T(2,128)(2,1)S(1)}, bf16[32,1,1024]{2,1,0:T(2,128)(2,1)S(1)}, u32[]{:S(2)}, u32[]{:S(2)}) collective-permute-start(bf16[32,1,1024]{2,1,0:T(2,128)(2,1)S(1)} %get-tuple-element.16), channel_id=1, source_target_pairs={{0,8},{8,16},{16,24},{1,9},{9,17},{17,25},{2,10},{10,18},{18,26},{... | collective-permute-start | bytes 196616 | tf_op jit(solution)/shard_map/ppermute | solution.py:18
  25.8 1.3 collective-permute-start.3
  27.1 1.8 convert_reduce_fusion
  28.9 1.3 reshape.42
  30.2 3.8 %copy.65 = bf16[1,32,4,16,64]{1,0,4,3,2:T(2,128)(2,1)} copy(bf16[1,32,4,16,64]{4,3,2,1,0:T(8,128)(2,1)S(1)} %reshape.42) | data formatting | bytes 524288 | tf_op jit(solution)/shard_map/reshape | solution.py:33
  34.1 0.4 pad_maximum_fusion
  34.5 0.5 reshape.71
  35.1 1.7 copy.73
  36.8 0.3 pad.2.clone
  37.2 0.5 copy.60
  37.6 1.2 copy-done.2
  38.9 0.9 slice.32
  39.7 20.1 %all-gather.2.cloned.1.call-done = bf16[256,6,1024]{2,0,1:T(8,128)(2,1)} async-done(((bf16[32,6,1024]{2,0,1:T(8,128)(2,1)}), bf16[256,6,1024]{2,0,1:T(8,128)(2,1)}) %all-gather.2.cloned.1.call-update) | async-done | bytes 3145744 | tf_op jit(solution)/shard_map/all_gather | solution.py:47
  59.8 4.7 %copy.51 = bf16[256,6,1024]{0,2,1:T(8,128)(2,1)} copy(bf16[256,6,1024]{2,0,1:T(8,128)(2,1)} %all-gather.2.cloned.1.call-done) | data formatting | bytes 6291456 | tf_op jit(solution)/shard_map/all_gather | solution.py:47
  64.5 78.2 %fusion.1 = f32[3,3,3,256,32]{4,3,2,1,0:T(8,128)} fusion(bf16[1,32,4,16,64]{1,0,4,3,2:T(2,128)(2,1)S(1)} %copy-done.4, bf16[256,1,6,16,64]{0,4,3,2,1:T(8,128)(2,1)} %bitcast.38), kind=kOutput, calls=%fused_computation.2 | convolution fusion | flops 1718353920 | bytes 4292608 | tf_op jit(solution)/shard_map/transpose | solution.py:70
  142.7 3.1 %reshape.43 = f32[221184]{0:T(1024)S(1)} reshape(f32[3,3,3,256,32]{4,3,2,1,0:T(8,128)} %fusion.1) | data formatting | bytes 1769472 | tf_op jit(solution)/shard_map/reshape | solution.py:70
  145.8 1.0 maximum_multiply_fusion
  146.8 0.4 reduce-scatter.4.cloned.1.call-start
  147.3 4.1 %broadcast_select_fusion = f32[4,16,8,9,256]{4,2,3,1,0:T(8,128)S(1)} fusion(pred[8,9]{0,1:T(8,128)(4,1)S(1)} %copy-done.8, bf16[3,3,3,256,32]{3,4,2,1,0:T(8,128)(2,1)S(1)} %bitcast.34, bf16[32,6,16,1,7,2]{0,4,5,2,1,3:T(8,128)(2,1)S(1)} %copy-done.5, bf16[32,6,16,1,8,9]{0,4,5,2,1,3:T(8,128)(2,1)S(1)} %copy-done.3), kind=kOutput, calls=%fused_computation.13 | convolution fusion | flops 1956298752 | bytes 5689416 | tf_op jit(solution)/shard_map/conv_general_dilated | solution.py:78
  151.4 1.4 copy.61
  152.9 0.4 slice_bitcast_fusion
  153.3 4.4 %copy.62 = f32[1,256,4,16,64]{1,4,3,2,0:T(8,128)} copy(f32[1,256,4,16,64]{1,3,4,2,0:T(8,128)S(1)} %slice_bitcast_fusion) | data formatting | bytes 8388608 | tf_op jit(solution)/shard_map/conv_general_dilated | solution.py:78
  157.7 5.6 %copy.70 = f32[256,4096]{1,0:T(8,128)} copy(f32[256,4096]{0,1:T(8,128)} %bitcast.36) | data formatting | bytes 8388608
  163.4 3.9 %copy.72 = bf16[256,6,16,1,64]{0,2,4,1,3:T(8,128)(2,1)S(1)} copy(bf16[256,6,16,1,64]{0,4,2,1,3:T(8,128)(2,1)} %bitcast.39) | data formatting | bytes 6291456
  167.3 0.4 pad.clone
  167.7 1.5 copy.54
  169.2 0.2 slice.30
  169.4 17.4 %fusion.21 = f32[4,16,8,9,32]{4,2,3,1,0:T(8,128)S(1)} fusion(bf16[3,3,3,256,32]{3,4,2,1,0:T(8,128)(2,1)S(1)} %bitcast.33, bf16[256,6,16,1,7,2]{0,4,5,2,1,3:T(8,128)(2,1)S(1)} %slice.30, bf16[256,6,16,1,8,9]{0,4,5,2,1,3:T(8,128)(2,1)S(1)} %copy.54, pred[8,9]{0,1:T(8,128)(4,1)S(1)} %copy-done.8), kind=kOutput, calls=%fused_computation.22 | convolution fusion | flops 1966620672 | bytes 5259336 | tf_op jit(solution)/shard_map/conv_general_dilated | solution.py:50
  186.8 0.4 copy.55
  187.2 0.1 slice_bitcast_fusion.1
  187.4 2.0 copy.56
  189.4 1.6 reshape.38
  191.1 0.9 copy.67
  192.0 4.2 %all-reduce.2.cloned.1.call-done = f32[221216]{0:T(1024)} async-done(((f32[221216]{0:T(1024)}), f32[221216]{0:T(1024)}) %all-reduce.2.cloned.1.call-update) | async-done | bytes 884880 | tf_op jit(solution)/shard_map/psum | solution.py:72
  196.1 1.2 slice.34
  197.4 2.2 reshape.44
  199.6 3.3 %copy.69 = f32[27,256,32]{1,2,0:T(8,128)} copy(f32[27,256,32]{2,1,0:T(8,128)} %reshape.44) | data formatting | bytes 1769472
  202.9 1.2 slice.35
  204.0 44.8 %reduce-scatter.4.cloned.1.call-done = f32[32,4096]{1,0:T(8,128)} async-done(((f32[256,4096]{1,0:T(8,128)}), f32[32,4096]{1,0:T(8,128)}) %reduce-scatter.4.cloned.1.call-update) | async-done | bytes 524304
  248.9 1.5 copy.71
  250.4 1.2 copy.68
  (26 shorter events, 0.3 us)
Async XLA Ops:
  7.2 140.1 %copy-start = (bf16[27,256,32]{1,2,0:T(8,128)(2,1)S(1)}, bf16[27,256,32]{1,2,0:T(8,128)(2,1)}, u32[]{:S(2)}) copy-start(bf16[27,256,32]{1,2,0:T(8,128)(2,1)} %param.5) | copy-start | bytes 1327108
  7.2 26.9 %copy-start.1 = (bf16[32,4,1024]{2,1,0:T(4,128)(2,1)S(1)}, bf16[32,4,1024]{2,1,0:T(4,128)(2,1)}, u32[]{:S(2)}) copy-start(bf16[32,4,1024]{2,1,0:T(4,128)(2,1)} %param.7) | copy-start | bytes 786436
  7.2 52.6 %all-gather.2.cloned.1.call-start = ((), (), s32[]{:S(2)}) async-start(), calls=%async_computation.1 | async-start | bytes 3538944 | tf_op jit(solution)/shard_map/all_gather | solution.py:47
  8.4 6.7 %collective-permute-start = (bf16[32,1,1024]{2,0,1:T(8,128)(2,1)S(1)}, bf16[32,1,1024]{2,0,1:T(8,128)(2,1)S(1)}, u32[]{:S(2)}, u32[]{:S(2)}) collective-permute-start(bf16[32,1,1024]{2,0,1:T(8,128)(2,1)S(1)} %get-tuple-element.18), channel_id=1, source_target_pairs={{0,8},{8,16},{16,24},{1,9},{9,17},{17,25},{2,10},{10,18},{18,26},{... | collective-permute-start | bytes 196616 | tf_op jit(solution)/shard_map/ppermute | solution.py:18
  13.2 6.2 %collective-permute-start.1 = (bf16[32,1,1024]{2,0,1:T(8,128)(2,1)S(1)}, bf16[32,1,1024]{2,0,1:T(8,128)(2,1)S(1)}, u32[]{:S(2)}, u32[]{:S(2)}) collective-permute-start(bf16[32,1,1024]{2,0,1:T(8,128)(2,1)S(1)} %get-tuple-element.19), channel_id=1, source_target_pairs={{8,0},{16,8},{24,16},{9,1},{17,9},{25,17},{10,2},{18,10},{26,18},{... | collective-permute-start | bytes 196616 | tf_op jit(solution)/shard_map/ppermute | solution.py:19
  20.2 175.9 %all-reduce.2.cloned.1.call-start = ((), (), s32[]{:S(2)}) async-start(), calls=%async_computation.2 | async-start | bytes 1777664 | tf_op jit(solution)/shard_map/psum | solution.py:72
  21.5 12.6 %collective-permute-start.2 = (bf16[32,1,1024]{2,1,0:T(2,128)(2,1)S(1)}, bf16[32,1,1024]{2,1,0:T(2,128)(2,1)S(1)}, u32[]{:S(2)}, u32[]{:S(2)}) collective-permute-start(bf16[32,1,1024]{2,1,0:T(2,128)(2,1)S(1)} %get-tuple-element.16), channel_id=1, source_target_pairs={{0,8},{8,16},{16,24},{1,9},{9,17},{17,25},{2,10},{10,18},{18,26},{... | collective-permute-start | bytes 196616 | tf_op jit(solution)/shard_map/ppermute | solution.py:18
  25.8 8.3 %collective-permute-start.3 = (bf16[32,1,1024]{2,1,0:T(2,128)(2,1)S(1)}, bf16[32,1,1024]{2,1,0:T(2,128)(2,1)S(1)}, u32[]{:S(2)}, u32[]{:S(2)}) collective-permute-start(bf16[32,1,1024]{2,1,0:T(2,128)(2,1)S(1)} %get-tuple-element.17), channel_id=1, source_target_pairs={{8,0},{16,8},{24,16},{9,1},{17,9},{25,17},{10,2},{18,10},{26,18},{... | collective-permute-start | bytes 196616 | tf_op jit(solution)/shard_map/ppermute | solution.py:19
  37.6 1.3 copy-start.2
  38.9 25.6 %copy-start.4 = (bf16[1,32,4,16,64]{1,0,4,3,2:T(2,128)(2,1)S(1)}, bf16[1,32,4,16,64]{1,0,4,3,2:T(2,128)(2,1)}, u32[]{:S(2)}) copy-start(bf16[1,32,4,16,64]{1,0,4,3,2:T(2,128)(2,1)} %copy.65) | copy-start | bytes 786436
  142.7 3.1 %copy-start.6 = (f32[32]{0:T(128)S(1)}, f32[32]{0:T(128)}, u32[]{:S(2)}) copy-start(f32[32]{0:T(128)} %convert_reduce_fusion) | copy-start | bytes 388
  142.7 4.6 %copy-start.3 = (bf16[32,6,16,1,8,9]{0,4,5,2,1,3:T(8,128)(2,1)S(1)}, bf16[32,6,16,1,8,9]{0,4,5,2,1,3:T(8,128)(2,1)}, u32[]{:S(2)}) copy-start(bf16[32,6,16,1,8,9]{0,4,5,2,1,3:T(8,128)(2,1)} %copy-done.2) | copy-start | bytes 1327108
  142.7 4.7 %copy-start.5 = (bf16[32,6,16,1,7,2]{0,4,5,2,1,3:T(8,128)(2,1)S(1)}, bf16[32,6,16,1,7,2]{0,4,5,2,1,3:T(8,128)(2,1)}, u32[]{:S(2)}) copy-start(bf16[32,6,16,1,7,2]{0,4,5,2,1,3:T(8,128)(2,1)} %slice.32) | copy-start | bytes 258052
  142.7 4.7 %copy-start.8 = (pred[8,9]{0,1:T(8,128)(4,1)S(1)}, pred[8,9]{0,1:T(8,128)(4,1)}, u32[]{:S(2)}) copy-start(pred[8,9]{0,1:T(8,128)(4,1)} %constant.12) | copy-start | bytes 220
  146.8 102.0 %reduce-scatter.4.cloned.1.call-start = ((), (), s32[]{:S(2)}) async-start(), calls=%async_computation.3 | async-start | bytes 4718592
  187.2 3.7 %copy-start.7 = (f32[32]{0:T(128)S(1)}, f32[32]{0:T(128)}, u32[]{:S(2)}) copy-start(f32[32]{0:T(128)} %param.6) | copy-start | bytes 388
Sparse Core Ops, SparseCore 0:
  20.3 39.4 all-gather.1
  147.0 49.1 all-reduce.1
  198.5 50.2 reduce-scatter.3

commit v2 on v0

--- a/solution.py
+++ b/solution.py
@@ -51,6 +51,32 @@
     return jnp.concatenate([rims[:, :1], field, rims[:, 3:]], axis=1)
 
 
+def all_reduce_pairs(flat, axis):
+    devices = lax.axis_size(axis)
+    steps = devices.bit_length() - 1
+    assert 1 << steps == devices
+    length = flat.shape[0]
+    padded_length = -(-length // devices) * devices
+    current = jnp.pad(flat, (0, padded_length - length))
+    index = lax.axis_index(axis)
+    for step in range(steps):
+        half = current.shape[0] // 2
+        bit = (index >> step) & 1
+        keep = lax.dynamic_slice_in_dim(current, bit * half, half)
+        send = lax.dynamic_slice_in_dim(current, (1 - bit) * half, half)
+        pairs = [(i, i ^ (1 << step)) for i in range(devices)]
+        current = keep + lax.ppermute(send, axis, pairs)
+    for step in reversed(range(steps)):
+        half = current.shape[0]
+        bit = (index >> step) & 1
+        pairs = [(i, i ^ (1 << step)) for i in range(devices)]
+        other = lax.ppermute(current, axis, pairs)
+        both = jnp.zeros((2 * half,), current.dtype)
+        both = lax.dynamic_update_slice_in_dim(both, current, bit * half, 0)
+        current = lax.dynamic_update_slice_in_dim(both, other, (1 - bit) * half, 0)
+    return current[:length]
+
+
 def body(inputs, weight, bias_term, output_grad):
     taps_total = weight.shape[0]
     channels_in = weight.shape[1]
@@ -95,7 +121,10 @@
         * grad_scale
     )
     bias_part = jnp.sum(output_grad.astype(jnp.float32), axis=(1, 2)) * grad_scale
-    weight_grad, bias_grad = lax.psum((weight_part, bias_part), "space")
+    weight_size = weight_part.size
+    reduced = all_reduce_pairs(jnp.concatenate([weight_part.reshape(weight_size), bias_part]), "space")
+    weight_grad = reduced[:weight_size].reshape(weight_part.shape)
+    bias_grad = reduced[weight_size : weight_size + bias_part.shape[0]]
     spread = jnp.stack(
         [
             shift_cells(

time: 215 us -> 191 us (0.89)
  other arithmetic: 44.8 us -> 26.1 us
  local copies, waits for them, and re-layouts: 71.1 us -> 89.2 us
  waiting for transfers between devices: 37.5 us -> 21.3 us
  blocking collectives: 10.9 us -> 0 us
  starting transfers between devices: 12.9 us -> 16.6 us
    psum x1 -> x0, waiting for transfers between devices: 37.4 us -> none  [body(): weight_grad, bias_grad = lax.psum((weight_part, bias_part), 'space')]
    unnamed x53 -> x52, other arithmetic: 30.5 us -> 10.9 us
    all_gather x1, waiting for transfers between devices: 0.01 us -> 19 us  [body(): gathered = lax.all_gather(rimmed, 'chan', axis=0, tiled=True)]
    psum x1 -> x0, blocking collectives: 10.9 us -> none  [body(): weight_grad, bias_grad = lax.psum((weight_part, bias_part), 'space')]
    dynamic_update_slice x0 -> x3, local copies, waits for them, and re-layouts: none -> 9.16 us  [the longest x2 6.18 us: all_reduce_pairs(): current = lax.dynamic_update_slice_in_dim(both, other, (1 - bit) * half, 0)]
    reshape x0 -> x2, local copies, waits for them, and re-layouts: none -> 5.11 us  [the longest x1 2.92 us: body(): weight_part.reshape(weight_size)]
    ppermute x0 -> x4, starting transfers between devices: none -> 4.34 us  [the longest x2 3.1 us: all_reduce_pairs(): current = keep + lax.ppermute(send, axis, pairs)]
    dot_general x1, matrix products: 7.58 us -> 4.48 us  [body(): jnp.dot(backward_weight, spread, preferred_element_type=jnp.float32)]
  transfers between devices with their start and end apart: 7 -> 10, of which waited for: 1 -> 2; matrix products, arithmetic and copies ran while one was open for 62% -> 68% of each run, Pallas kernels for 0% -> 0%
where the time goes in v2:
time: 191 us; the launch traced here: 190 us
  local copies, waits for them, and re-layouts  89.2 us (47%)
  other arithmetic  26.1 us (14%)
  matrix products  22 us (12%)
  waiting for transfers between devices  21.3 us (11%)
  starting transfers between devices  16.6 us (9%)
  between operations  14.6 us (8%)
    reshape x1, local copies, waits for them, and re-layouts, body(): stacked.reshape(taps_total, block_out, depth_cells + 2, plane_cells)  27.9 us
    unnamed x17, local copies, waits for them, and re-layouts  22.7 us
    all_gather x1, waiting for transfers between devices, body(): gathered = lax.all_gather(rimmed, 'chan', axis=0, tiled=True)  19 us
    squeeze x2, local copies, waits for them, and re-layouts, body(): stacked[tap_index, :, 1 + depth_step:1 + depth_step + depth_cells]  15.2 us
    unnamed x52, other arithmetic  10.9 us
    dot_general x1, matrix products, body(): jnp.dot(forward_weight, gathered_flat, preferred_element_type=jnp.float32)  10.8 us
    convert_element_type x1, other arithmetic, body(): outputs = (forward + bias_term[:, None, None]).astype(jnp.bfloat16)  10.3 us
    ppermute x2, starting transfers between devices, padded_2(): before = lax.ppermute(last, axis, up)  9.4 us
  transfers between devices with their start and end apart: 10, of which 2 were waited for; matrix products, arithmetic and copies ran while one was open for 68% of the time, Pallas kernels for 0%

profile of v2, /device:TPU:0, one launch (start us, length us, event | category | flops | bytes accessed | tf_op | source)
XLA Modules:
  0.0 189.7 jit_solution(9719931294279383408)
XLA Ops:
  7.2 1.1 copy.21
  8.3 4.8 %collective-permute-start = (bf16[32,1,1024]{2,0,1:T(8,128)(2,1)S(1)}, bf16[32,1,1024]{2,0,1:T(8,128)(2,1)S(1)}, u32[]{:S(2)}, u32[]{:S(2)}) collective-permute-start(bf16[32,1,1024]{2,0,1:T(8,128)(2,1)S(1)} %get-tuple-element.49), channel_id=1, source_target_pairs={{0,8},{8,16},{16,24},{1,9},{9,17},{17,25},{2,10},{10,18},{18,26},{... | collective-permute-start | bytes 196616 | tf_op jit(solution)/shard_map/ppermute | solution.py:28
  13.2 1.3 collective-permute-start.1
  14.5 1.3 fusion.154
  15.7 4.6 %collective-permute-start.3 = (bf16[32,1,1024]{2,1,0:T(2,128)(2,1)S(1)}, bf16[32,1,1024]{2,1,0:T(2,128)(2,1)S(1)}, u32[]{:S(2)}, u32[]{:S(2)}) collective-permute-start(bf16[32,1,1024]{2,1,0:T(2,128)(2,1)S(1)} %get-tuple-element.47), channel_id=1, source_target_pairs={{0,8},{8,16},{16,24},{1,9},{9,17},{17,25},{2,10},{10,18},{18,26},{... | collective-permute-start | bytes 196616 | tf_op jit(solution)/shard_map/ppermute | solution.py:28
  20.3 1.3 collective-permute-start.2
  21.6 1.3 convert_reduce_fusion
  22.9 1.0 copy.25
  28.8 4.0 %copy-done.3 = bf16[27,32,6,1024]{3,1,2,0:T(8,128)(2,1)} copy-done((bf16[27,32,6,1024]{3,1,2,0:T(8,128)(2,1)}, bf16[27,32,6,1024]{3,1,2,0:T(8,128)(2,1)S(1)}, u32[]{:S(2)}) %copy-start.3) | copy-done | bytes 10616856
  32.8 0.8 pad_maximum_fusion
  33.9 0.6 pad_maximum_fusion.1
  35.7 0.3 bitcast_dynamic-update-slice_fusion.24
  36.2 0.3 bitcast_dynamic-update-slice_fusion.22
  36.5 0.3 bitcast_dynamic-update-slice_fusion.21
  38.0 0.3 bitcast_dynamic-update-slice_fusion.15
  38.3 0.3 bitcast_dynamic-update-slice_fusion.14
  38.8 0.3 bitcast_dynamic-update-slice_fusion.12
  40.3 0.3 bitcast_dynamic-update-slice_fusion.6
  40.9 0.3 bitcast_dynamic-update-slice_fusion.4
  41.4 4.9 %copy.32 = bf16[108,8,4,1024]{3,1,2,0:T(8,128)(2,1)S(1)} copy(bf16[108,8,4,1024]{3,2,1,0:T(4,128)(2,1)S(1)} %bitcast.273) | data formatting | bytes 14155776
  46.3 4.5 %convolution_bitcast_fusion.1 = f32[256,4096]{0,1:T(8,128)} fusion(bf16[864,4096]{1,0:T(8,128)(2,1)S(1)} %bitcast.274, bf16[256,864]{0,1:T(8,128)(2,1)S(1)} %bitcast.271), kind=kOutput, calls=%fused_computation.1 | convolution fusion | flops 1811939328 | bytes 11714560 | tf_op jit(solution)/shard_map/dot_general | solution.py:141
  50.7 5.6 %copy.30 = f32[256,4096]{1,0:T(8,128)} copy(f32[256,4096]{0,1:T(8,128)} %convolution_bitcast_fusion.1) | data formatting | bytes 8388608
  56.4 19.0 %all-gather.2.cloned.1.call-done = bf16[256,6,1024]{2,0,1:T(8,128)(2,1)} async-done(((bf16[32,6,1024]{2,0,1:T(8,128)(2,1)}), bf16[256,6,1024]{2,0,1:T(8,128)(2,1)}) %all-gather.2.cloned.1.call-update) | async-done | bytes 3145744 | tf_op jit(solution)/shard_map/all_gather | solution.py:90
  75.4 6.7 %fusion.8 = f32[27,256,32]{1,2,0:T(8,128)S(1)} fusion(bf16[27,32,6,1024]{3,1,2,0:T(8,128)(2,1)} %copy-done.3, bf16[256,6,1024]{2,0,1:T(8,128)(2,1)} %all-gather.2.cloned.1.call-done), kind=kOutput, calls=%fused_computation.6 | convolution fusion | flops 2718130176 | bytes 14647296 | tf_op jit(solution)/shard_map/dot_general | solution.py:116
  82.1 2.4 %copy.26 = f32[27,256,32]{2,1,0:T(8,128)} copy(f32[27,256,32]{1,2,0:T(8,128)S(1)} %fusion.8) | data formatting | bytes 1769472 | tf_op jit(solution)/shard_map/mul | solution.py:120
  84.4 2.9 %reshape.43 = f32[221184]{0:T(1024)S(1)} reshape(f32[27,256,32]{2,1,0:T(8,128)} %copy.26) | data formatting | bytes 1769472 | tf_op jit(solution)/shard_map/reshape | solution.py:125
  87.4 0.3 fusion.64
  87.7 1.6 collective-permute-start.4
  89.3 4.7 %copy.24 = bf16[256,6,1024]{0,2,1:T(8,128)(2,1)} copy(bf16[256,6,1024]{2,0,1:T(8,128)(2,1)} %all-gather.2.cloned.1.call-done) | data formatting | bytes 6291456 | tf_op jit(solution)/shard_map/all_gather | solution.py:90
  93.9 10.8 %convolution_bitcast_fusion = f32[864,6144]{1,0:T(8,128)} fusion(bf16[256,6144]{0,1:T(8,128)(2,1)} %bitcast.272, bf16[864,256]{1,0:T(8,128)(2,1)S(1)} %bitcast.270), kind=kOutput, calls=%fused_computation | convolution fusion | flops 2717908992 | bytes 24821760 | tf_op jit(solution)/shard_map/dot_general | solution.py:93
  104.7 27.9 %reshape.39 = f32[27,32,6,1024]{3,2,1,0:T(8,128)} reshape(f32[864,6144]{1,0:T(8,128)} %convolution_bitcast_fusion) | data formatting | bytes 42467328 | tf_op jit(solution)/shard_map/reshape | solution.py:94
  132.6 0.3 fusion.66
  133.0 1.5 collective-permute-start.5
  134.6 10.9 %slice_bitcast_fusion.26 = (f32[32,4,1024]{2,1,0:T(4,128)S(1)}, f32[32,4,1024]{2,1,0:T(4,128)S(1)}, f32[32,4,1024]{2,1,0:T(4,128)S(1)}, f32[32,4,1024]{2,1,0:T(4...) fusion(f32[27,32,6,1024]{3,2,1,0:T(8,128)} %reshape.39), kind=kLoop, calls=%fused_computation.117 | loop fusion | bytes 19922944 | tf_op jit(solution)/shard_map/squeeze | solution.py:98
  145.6 1.1 fusion.153
  146.7 0.6 collective-permute-start.6
  147.3 4.3 %slice_bitcast_fusion.25 = (f32[32,4,1024]{2,1,0:T(4,128)}, f32[32,4,1024]{2,1,0:T(4,128)}, f32[32,4,1024]{2,1,0:T(4,128)}, f32[32,4,1024]{2,1,0:T(4,128)}, f32[32,4,1024]{2,1,0:T(4,128)}) fusion(f32[27,32,6,1024]{3,2,1,0:T(8,128)} %reshape.39), kind=kLoop, calls=%fused_computation.116 | loop fusion | bytes 5242880 | tf_op jit(solution)/shard_map/squeeze | solution.py:98
  151.6 2.2 %collective-permute-done.6 = f32[55304]{0:T(1024)S(1)} collective-permute-done((f32[55304]{0:T(1024)S(1)}, f32[55304]{0:T(1024)S(1)}, u32[]{:S(2)}, u32[]{:S(2)}) %collective-permute-start.6) | collective-permute-done | bytes 221248 | tf_op jit(solution)/shard_map/ppermute | solution.py:73
  153.8 1.5 dynamic_update_slice.13
  155.4 0.6 collective-permute-start.7
  156.0 10.3 %add_convert_fusion = bf16[32,4,1024]{2,1,0:T(4,128)(2,1)} fusion(f32[32,4,1024]{2,1,0:T(4,128)} %get-tuple-element.39, f32[32,4,1024]{2,1,0:T(4,128)} %get-tuple-element.29, f32[32,4,1024]{2,1,0:T(4,128)S(1)} %get-tuple-element.19, f32[32,4,1024]{2,1,0:T(4,128)S(1)} %get-tuple-element.20, f32[27,32,6,1024]{3,2,1,0:T(8,128)} %reshape.39, ...), kind=kLoop, calls=%fused_computation.119 | loop fusion | flops 7208960 | bytes 14421120 | tf_op jit(solution)/shard_map/convert_element_type | solution.py:102
  166.3 3.0 %dynamic_update_slice.14 = f32[221216]{0:T(1024)S(1)} dynamic-update-slice(f32[221216]{0:T(1024)S(1)} %broadcast_in_dim.256, f32[110608]{0:T(1024)S(1)} %dynamic_update_slice.13, s32[]{:T(128)S(6)} %select_n.671) | dynamic-update-slice | bytes 884868 | tf_op jit(solution)/shard_map/dynamic_update_slice | solution.py:75
  169.3 4.7 %dynamic_update_slice.15 = f32[221216]{0:T(1024)S(1)} dynamic-update-slice(f32[221216]{0:T(1024)S(1)} %dynamic_update_slice.14, f32[110608]{0:T(1024)} %collective-permute-done.7, s32[]{:T(128)S(6)} %select_n.672) | dynamic-update-slice | bytes 884868 | tf_op jit(solution)/shard_map/dynamic_update_slice | solution.py:76
  174.0 0.5 slice.521
  174.6 2.2 %reshape.44 = f32[27,256,32]{2,1,0:T(8,128)} reshape(f32[221184]{0:T(1024)S(1)} %slice.520) | data formatting | bytes 1769472 | tf_op jit(solution)/shard_map/reshape | solution.py:126
  176.8 3.3 %copy.28 = f32[27,256,32]{1,2,0:T(8,128)} copy(f32[27,256,32]{2,1,0:T(8,128)} %reshape.44) | data formatting | bytes 1769472
  180.1 1.5 copy.31
  181.6 1.2 copy.27
  (76 shorter events, 9.9 us)
Async XLA Ops:
  7.2 39.1 %copy-start = (bf16[27,256,32]{1,2,0:T(8,128)(2,1)S(1)}, bf16[27,256,32]{1,2,0:T(8,128)(2,1)}, u32[]{:S(2)}) copy-start(bf16[27,256,32]{1,2,0:T(8,128)(2,1)} %param.5) | copy-start | bytes 1327108
  7.2 68.2 %all-gather.2.cloned.1.call-start = ((), (), s32[]{:S(2)}) async-start(), calls=%async_computation.1 | async-start | bytes 3538944 | tf_op jit(solution)/shard_map/all_gather | solution.py:90
  8.3 24.5 %collective-permute-start = (bf16[32,1,1024]{2,0,1:T(8,128)(2,1)S(1)}, bf16[32,1,1024]{2,0,1:T(8,128)(2,1)S(1)}, u32[]{:S(2)}, u32[]{:S(2)}) collective-permute-start(bf16[32,1,1024]{2,0,1:T(8,128)(2,1)S(1)} %get-tuple-element.49), channel_id=1, source_target_pairs={{0,8},{8,16},{16,24},{1,9},{9,17},{17,25},{2,10},{10,18},{18,26},{... | collective-permute-start | bytes 196616 | tf_op jit(solution)/shard_map/ppermute | solution.py:28
  13.2 19.6 %collective-permute-start.1 = (bf16[32,1,1024]{2,0,1:T(8,128)(2,1)S(1)}, bf16[32,1,1024]{2,0,1:T(8,128)(2,1)S(1)}, u32[]{:S(2)}, u32[]{:S(2)}) collective-permute-start(bf16[32,1,1024]{2,0,1:T(8,128)(2,1)S(1)} %get-tuple-element.50), channel_id=1, source_target_pairs={{8,0},{16,8},{24,16},{9,1},{17,9},{25,17},{10,2},{18,10},{26,18},{... | collective-permute-start | bytes 196616 | tf_op jit(solution)/shard_map/ppermute | solution.py:29
  15.7 18.1 %collective-permute-start.3 = (bf16[32,1,1024]{2,1,0:T(2,128)(2,1)S(1)}, bf16[32,1,1024]{2,1,0:T(2,128)(2,1)S(1)}, u32[]{:S(2)}, u32[]{:S(2)}) collective-permute-start(bf16[32,1,1024]{2,1,0:T(2,128)(2,1)S(1)} %get-tuple-element.47), channel_id=1, source_target_pairs={{0,8},{8,16},{16,24},{1,9},{9,17},{17,25},{2,10},{10,18},{18,26},{... | collective-permute-start | bytes 196616 | tf_op jit(solution)/shard_map/ppermute | solution.py:28
  20.3 13.6 %collective-permute-start.2 = (bf16[32,1,1024]{2,1,0:T(2,128)(2,1)S(1)}, bf16[32,1,1024]{2,1,0:T(2,128)(2,1)S(1)}, u32[]{:S(2)}, u32[]{:S(2)}) collective-permute-start(bf16[32,1,1024]{2,1,0:T(2,128)(2,1)S(1)} %get-tuple-element.48), channel_id=1, source_target_pairs={{8,0},{16,8},{24,16},{9,1},{17,9},{25,17},{10,2},{18,10},{26,18},{... | collective-permute-start | bytes 196616 | tf_op jit(solution)/shard_map/ppermute | solution.py:29
  25.8 8.1 %copy-start.2 = (bf16[32,4,1024]{2,1,0:T(4,128)(2,1)S(1)}, bf16[32,4,1024]{2,1,0:T(4,128)(2,1)}, u32[]{:S(2)}) copy-start(bf16[32,4,1024]{2,1,0:T(4,128)(2,1)} %param.7) | copy-start | bytes 786436
  28.8 4.0 %copy-start.3 = (bf16[27,32,6,1024]{3,1,2,0:T(8,128)(2,1)}, bf16[27,32,6,1024]{3,1,2,0:T(8,128)(2,1)S(1)}, u32[]{:S(2)}) copy-start(bf16[27,32,6,1024]{3,1,2,0:T(8,128)(2,1)S(1)} %fusion.138) | copy-start | bytes 31850500
  33.6 146.4 %reduce-scatter.4.cloned.1.call-start = ((), (), s32[]{:S(2)}) async-start(), calls=%async_computation.2 | async-start | bytes 4718592
  87.7 44.9 %collective-permute-start.4 = (f32[110608]{0:T(1024)S(1)}, f32[110608]{0:T(1024)S(1)}, u32[]{:S(2)}, u32[]{:S(2)}) collective-permute-start(f32[110608]{0:T(1024)S(1)} %fusion.64), channel_id=1, source_target_pairs={{0,8},{8,0},{16,24},{24,16},{1,9},{9,1},{17,25},{25,17},{2,10},{10... | collective-permute-start | bytes 1327304 | tf_op jit(solution)/shard_map/ppermute | solution.py:68
  133.0 12.5 %collective-permute-start.5 = (f32[55304]{0:T(1024)S(1)}, f32[55304]{0:T(1024)S(1)}, u32[]{:S(2)}, u32[]{:S(2)}) collective-permute-start(f32[55304]{0:T(1024)S(1)} %dynamic_slice.15), channel_id=1, source_target_pairs={{0,16},{8,24},{16,0},{24,8},{1,17},{9,25},{17,1},{25,9},{2,18},{10... | collective-permute-start | bytes 663656 | tf_op jit(solution)/shard_map/ppermute | solution.py:68
  145.5 10.5 %copy-start.4 = (f32[32]{0:T(128)S(1)}, f32[32]{0:T(128)}, u32[]{:S(2)}) copy-start(f32[32]{0:T(128)} %param.6) | copy-start | bytes 388
  146.7 7.1 %collective-permute-start.6 = (f32[55304]{0:T(1024)S(1)}, f32[55304]{0:T(1024)S(1)}, u32[]{:S(2)}, u32[]{:S(2)}) collective-permute-start(f32[55304]{0:T(1024)S(1)} %get-tuple-element.17), channel_id=1, source_target_pairs={{0,16},{8,24},{16,0},{24,8},{1,17},{9,25},{17,1},{25,9},{2,18},{10... | collective-permute-start | bytes 663656 | tf_op jit(solution)/shard_map/ppermute | solution.py:73
  155.4 14.0 %collective-permute-start.7 = (f32[110608]{0:T(1024)S(1)}, f32[110608]{0:T(1024)}, u32[]{:S(2)}, u32[]{:S(2)}) collective-permute-start(f32[110608]{0:T(1024)S(1)} %dynamic_update_slice.13), channel_id=1, source_target_pairs={{0,8},{8,0},{16,24},{24,16},{1,9},{9,1},{17,25},{25,17},{2,10},{10... | collective-permute-start | bytes 1327304 | tf_op jit(solution)/shard_map/ppermute | solution.py:73
  166.3 16.5 %copy-start.1 = (bf16[27,256,32]{1,2,0:T(8,128)(2,1)S(1)}, bf16[27,256,32]{1,2,0:T(8,128)(2,1)}, u32[]{:S(2)}) copy-start(bf16[27,256,32]{1,2,0:T(8,128)(2,1)} %param.5) | copy-start | bytes 1327108
Sparse Core Ops, SparseCore 0:
  33.8 41.5 all-gather.1
  77.6 48.8 reduce-scatter.3
